TPU v7x, 256 devices: a whole 4x4x8 slice. The times are simulated.
256 devices in a mesh: scen: 64 (over y, x, z_hi, core), trade: 4 (over z_lo).
Axes of the slice: x: 4, y: 4, z: 8 (z_hi: 2, z_lo: 4; z = z_hi * 4 + z_lo), core: 2. Of those that a mesh axis runs over, the one named last changes fastest.
Arguments:
- payoffs: float32 [12, 12, 12, 4, 8192], P(None, None, None, 'trade', 'scen'), may hold values from -4 to 4
- sweep_counts: int32 [4, 8192], P('trade', 'scen'), may hold values from 1 to 6
- netting_map: int32 [4, 8192], P('trade'), may hold values from 0 to 511
- type_lengths: int32 [8], replicated, may hold values from 1 to 8192, 32768 in all
- type_diffusion: float32 [8], replicated, may hold values from 0.02 to 0.15
- type_discount: float32 [8], replicated, may hold values from 0.01 to 0.12
- factors: float32 [3, 8192], P(None, 'scen'), may hold values from -1 to 1
Outputs:
- exposures: float32 [8192, 512], P('scen', 'trade')
- allocation: float32 [4, 8192], P('trade', 'scen')
All inputs are finite; a program needn't handle non-finite values.
Results may differ from a plain program's by a relative error of at most 0.0055.
Values may be sent and summed in bfloat16 or wider, within the bound.
No kernel may reach another device: no remote copies, remote signals or barrier semaphores. Data moves between devices by JAX's collectives and lax.ppermute only.
A program may use at most 128 MiB of HBM per device.

v0:
```python
import jax
import jax.numpy as jnp
from jax import lax
from jax.sharding import PartitionSpec as P

GRID = 12
NETS = 512
TYPES = 8
MAX_SWEEPS = 6


def cheb_matrix():
    intervals = GRID - 1
    order_index = jnp.arange(GRID, dtype=jnp.float32)
    end_weights = jnp.where((order_index == 0) | (order_index == intervals), 0.5, 1.0).astype(
        jnp.float32
    )
    angles = jnp.pi * order_index[:, None] * order_index[None, :] / intervals
    return 2.0 / intervals * end_weights[:, None] * end_weights[None, :] * jnp.cos(angles)


def cheb_basis(factors):
    factor_basis = []
    for column in range(3):
        point = factors[column]
        recurrence = [jnp.ones_like(point), point]
        for degree in range(2, GRID):
            recurrence.append(2.0 * point * recurrence[-1] - recurrence[-2])
        factor_basis.append(jnp.stack(recurrence[:GRID], 0))
    product = factor_basis[0][:, None, None, :] * factor_basis[1][None, :, None, :]
    product = product * factor_basis[2][None, None, :, :]
    return product.reshape(GRID * GRID * GRID, -1).astype(jnp.bfloat16)


def price(grid_values, counts, trade_index, type_lengths, type_diffusion, type_discount):
    type_ends = jnp.cumsum(type_lengths)
    type_ids = jnp.sum((trade_index[:, None] >= type_ends[None, :]).astype(jnp.int32), axis=1)
    type_hot = (type_ids[:, None] == jnp.arange(TYPES, dtype=jnp.int32)[None, :]).astype(
        jnp.float32
    )
    diffusion = jnp.sum(type_hot * type_diffusion[None, :], axis=1)
    discount = jnp.sum(type_hot * type_discount[None, :], axis=1)

    def smooth_step(degree, field):
        padded = jnp.pad(field, ((1, 1), (1, 1), (1, 1), (0, 0)))
        beside = padded[2:, 1:-1, 1:-1] + padded[:-2, 1:-1, 1:-1]
        beside = beside + padded[1:-1, 2:, 1:-1] + padded[1:-1, :-2, 1:-1]
        beside = beside + padded[1:-1, 1:-1, 2:] + padded[1:-1, 1:-1, :-2]
        updated = field + diffusion * (beside - 6.0 * field) - discount * field
        return jnp.where(degree < counts, updated, field)

    field = lax.fori_loop(0, MAX_SWEEPS, smooth_step, grid_values)
    matrix = cheb_matrix()
    field = jnp.einsum("ai,ijlp->ajlp", matrix, field, precision=lax.Precision.HIGHEST)
    field = jnp.einsum("bj,ajlp->ablp", matrix, field, precision=lax.Precision.HIGHEST)
    field = jnp.einsum("cl,ablp->abcp", matrix, field, precision=lax.Precision.HIGHEST)
    return field.reshape(GRID * GRID * GRID, -1).astype(jnp.bfloat16)


def shards(
    payoffs, sweep_counts, netting_map, type_lengths, type_diffusion, type_discount, factors
):
    trades_here = payoffs.shape[4]
    scen_index = lax.axis_index("scen")
    group_index = lax.axis_index("trade")
    block_size = trades_here * lax.axis_size("scen")
    first_trade = group_index * block_size + scen_index * trades_here
    trade_index = first_trade + jnp.arange(trades_here, dtype=jnp.int32)
    coef_local = price(
        payoffs[:, :, :, 0, :],
        sweep_counts[0],
        trade_index,
        type_lengths,
        type_diffusion,
        type_discount,
    )
    own_sets = lax.dynamic_slice_in_dim(netting_map[0], scen_index * trades_here, trades_here)
    coef_rows = lax.all_gather(coef_local, "trade", axis=1, tiled=True)
    set_ids = lax.all_gather(own_sets, "trade", axis=0, tiled=True)
    sets_here = NETS // lax.axis_size("trade")
    classes = group_index * sets_here + jnp.arange(sets_here, dtype=jnp.int32)
    set_hot = (set_ids[:, None] == classes[None, :]).astype(jnp.bfloat16)
    set_part = jnp.dot(coef_rows, set_hot, preferred_element_type=jnp.float32)
    set_coef = lax.psum(set_part, "scen")
    basis_rows = cheb_basis(factors).astype(jnp.float32)
    totals = lax.dot_general(
        basis_rows, set_coef, (((0,), (0,)), ((), ())), precision=lax.Precision.HIGHEST
    )
    exposures = jnp.maximum(totals, 0.0)
    scen_total = factors.shape[1] * lax.axis_size("scen")
    weight_part = jnp.dot(basis_rows, exposures, precision=lax.Precision.HIGHEST)
    weights = lax.psum(weight_part, "scen") / scen_total
    trade_weights = lax.dot_general(
        coef_rows.astype(jnp.float32),
        weights,
        (((0,), (0,)), ((), ())),
        precision=lax.Precision.HIGHEST,
    )
    alloc_terms = jnp.sum(trade_weights * set_hot.astype(jnp.float32), axis=1)
    allocation = lax.psum_scatter(alloc_terms, "trade", scatter_dimension=0, tiled=True)
    return (exposures, allocation.reshape(1, trades_here))


def solution(mesh):
    return jax.shard_map(
        shards,
        mesh=mesh,
        in_specs=(
            P(None, None, None, "trade", "scen"),
            P("trade", "scen"),
            P("trade", None),
            P(),
            P(),
            P(),
            P(None, "scen"),
        ),
        out_specs=(P("scen", "trade"), P("trade", "scen")),
        check_vma=False,
    )
```

profile of v0, /device:TPU:0, one launch (start us, length us, event | category | flops | bytes accessed | tf_op | source)
XLA Modules:
  0.0 1643.2 jit_solution(8168996887689070114)
XLA Ops:
  7.3 0.8 reduce-window.8
  8.1 1.3 copy.21
  9.6 5.0 while.15
  9.6 0.1 copy.31
  9.8 0.7 fusion.49
  10.5 0.1 copy.31
  10.6 0.7 fusion.49
  11.3 0.1 copy.31
  11.4 0.7 fusion.49
  12.1 0.1 copy.31
  12.3 0.7 fusion.49
  13.0 0.1 copy.31
  13.1 0.7 fusion.49
  13.8 0.1 copy.31
  13.9 0.7 fusion.49
  14.6 1.6 fusion.13
  16.2 1.7 convolution_bitcast_fusion
  18.0 1.5 fusion.10
  19.5 0.9 convert_element_type.40
  20.5 10.5 all-gather
  31.0 37.2 %all-gather.3.cloned.1.call-done = bf16[1728,512]{1,0:T(8,128)(2,1)} async-done(((bf16[1728,128]{1,0:T(8,128)(2,1)}), bf16[1728,512]{1,0:T(8,128)(2,1)}) %all-gather.3.cloned.1.call-update) | async-done | bytes 1769488 | tf_op jit(solution)/shard_map/all_gather | solution.py:78
  68.2 3.1 fusion.18
  71.6 0.1 multiply_convert_fusion
  71.7 0.1 convert_element_type.36
  71.8 773.6 %all-reduce.5.cloned.1.call-done = f32[1728,128]{1,0:T(8,128)} async-done(((f32[1728,128]{1,0:T(8,128)}), f32[1728,128]{1,0:T(8,128)}) %all-reduce.5.cloned.1.call-update) | async-done | bytes 884752 | tf_op jit(solution)/shard_map/psum | solution.py:84
  845.4 1.8 convolution_maximum_fusion
  847.3 1.4 fusion.41
  848.8 0.6 dynamic-slice.1
  850.0 772.2 %all-reduce.7.cloned.1.call-done = f32[1728,128]{1,0:T(8,128)} async-done(((f32[1728,128]{1,0:T(8,128)}), f32[1728,128]{1,0:T(8,128)}) %all-reduce.7.cloned.1.call-update) | async-done | bytes 884752 | tf_op jit(solution)/shard_map/psum | solution.py:92
  1622.2 2.2 fusion.15
  1624.5 11.6 all-reduce.1
  1636.0 0.6 dynamic-slice_bitcast_fusion
  (43 shorter events, 0.7 us)
Async XLA Ops:
  7.2 13.3 copy-start
  7.2 2.3 copy-start.5
  7.2 2.3 copy-start.4
  7.2 2.4 copy-start.6
  7.2 61.0 %all-gather.3.cloned.1.call-start = ((), (), s32[]{:S(2)}) async-start(), calls=%async_computation | async-start | bytes 2211840 | tf_op jit(solution)/shard_map/all_gather | solution.py:78
  19.5 11.5 copy-start.3
  20.4 825.0 %all-reduce.5.cloned.1.call-start = ((), (), s32[]{:S(2)}) async-start(), calls=%async_computation.1 | async-start | bytes 1769472 | tf_op jit(solution)/shard_map/psum | solution.py:84
  71.3 1550.9 %all-reduce.7.cloned.1.call-start = ((), (), s32[]{:S(2)}) async-start(), calls=%async_computation.2 | async-start | bytes 1769472 | tf_op jit(solution)/shard_map/psum | solution.py:92
  847.3 777.2 %copy-start.2 = (f32[128,128]{1,0:T(8,128)}, f32[128,128]{1,0:T(8,128)S(1)}, u32[]{:S(2)}) copy-start(f32[128,128]{1,0:T(8,128)S(1)} %convolution_maximum_fusion) | copy-start | bytes 196612
  847.3 1.5 copy-start.7
  847.3 774.9 %copy-start.1 = (bf16[1728,512]{1,0:T(8,128)(2,1)S(1)}, bf16[1728,512]{1,0:T(8,128)(2,1)}, u32[]{:S(2)}) copy-start(bf16[1728,512]{1,0:T(8,128)(2,1)} %all-gather.3.cloned.1.call-done) | copy-start | bytes 5308420
Sparse Core Ops, SparseCore 0:
  20.5 47.6 all-gather.2
  71.4 773.9 all-reduce.4
  848.9 773.2 all-reduce.6
where the time goes:
time: 1640 us
  waiting for transfers between devices  1580 us (96%)
  blocking collectives  22.1 us (1%)
    psum x1, waiting for transfers between devices, shards(): set_coef = lax.psum(set_part, 'scen')  774 us
    psum x1, waiting for transfers between devices, shards(): weights = lax.psum(weight_part, 'scen') / scen_total  772 us
    all_gather x1, waiting for transfers between devices, shards(): coef_rows = lax.all_gather(coef_local, 'trade', axis=1, tiled=True)  37.2 us
  transfers between devices with their start and end apart: 3, of which 3 were waited for; matrix products, arithmetic and copies ran while one was open for 0% of the time, Pallas kernels for 0%

commit v1 on v0

--- a/solution.py
+++ b/solution.py
@@ -89,7 +89,7 @@
     exposures = jnp.maximum(totals, 0.0)
     scen_total = factors.shape[1] * lax.axis_size("scen")
     weight_part = jnp.dot(basis_rows, exposures, precision=lax.Precision.HIGHEST)
-    weights = lax.psum(weight_part, "scen") / scen_total
+    weights = jnp.sum(lax.all_gather(weight_part, "scen"), axis=0) / scen_total
     trade_weights = lax.dot_general(
         coef_rows.astype(jnp.float32),
         weights,

time: 1640 us -> 1260 us (0.77)
  waiting for transfers between devices: 1580 us -> 1180 us
  other arithmetic: 5.28 us -> 23.1 us
    psum x1 -> x0, waiting for transfers between devices: 772 us -> none  [shards(): weights = lax.psum(weight_part, 'scen') / scen_total]
    all_gather x0 -> x1, waiting for transfers between devices: none -> 371 us  [shards(): weights = jnp.sum(lax.all_gather(weight_part, 'scen'), axis=0) / scen_total]
    reduce_sum x0 -> x1, other arithmetic: none -> 17.9 us  [shards(): weights = jnp.sum(lax.all_gather(weight_part, 'scen'), axis=0) / scen_total]
where the time goes in v1:
time: 1260 us
  waiting for transfers between devices  1180 us (94%)
  other arithmetic  23.1 us (2%)
  blocking collectives  18.8 us (1%)
  between operations  14.6 us (1%)
    psum x1, waiting for transfers between devices, shards(): set_coef = lax.psum(set_part, 'scen')  774 us
    all_gather x1, waiting for transfers between devices, shards(): weights = jnp.sum(lax.all_gather(weight_part, 'scen'), axis=0) / scen_total  371 us
    all_gather x1, waiting for transfers between devices, shards(): coef_rows = lax.all_gather(coef_local, 'trade', axis=1, tiled=True)  37.2 us
  transfers between devices with their start and end apart: 3, of which 3 were waited for; matrix products, arithmetic and copies ran while one was open for 0% of the time, Pallas kernels for 0%

profile of v1, /device:TPU:0, one launch (start us, length us, event | category | flops | bytes accessed | tf_op | source)
XLA Modules:
  0.0 1255.5 jit_solution(9175407273311447975)
XLA Ops:
  7.3 0.8 reduce-window.8
  8.1 1.3 copy.21
  9.6 5.0 while.15
  9.6 0.1 copy.30
  9.8 0.7 fusion.49
  10.5 0.1 copy.30
  10.6 0.7 fusion.49
  11.3 0.1 copy.30
  11.4 0.7 fusion.49
  12.1 0.1 copy.30
  12.3 0.7 fusion.49
  13.0 0.1 copy.30
  13.1 0.7 fusion.49
  13.8 0.1 copy.30
  13.9 0.7 fusion.49
  14.6 1.6 fusion.13
  16.2 1.7 convolution_bitcast_fusion
  18.0 1.5 fusion.10
  19.5 0.9 convert_element_type.40
  20.5 10.5 all-gather
  31.0 37.2 %all-gather.5.cloned.1.call-done = bf16[1728,512]{1,0:T(8,128)(2,1)} async-done(((bf16[1728,128]{1,0:T(8,128)(2,1)}), bf16[1728,512]{1,0:T(8,128)(2,1)}) %all-gather.5.cloned.1.call-update) | async-done | bytes 1769488 | tf_op jit(solution)/shard_map/all_gather | solution.py:78
  68.2 3.1 fusion.18
  71.6 0.1 multiply_convert_fusion
  71.8 774.1 %all-reduce.4.cloned.1.call-done = f32[1728,128]{1,0:T(8,128)} async-done(((f32[1728,128]{1,0:T(8,128)}), f32[1728,128]{1,0:T(8,128)}) %all-reduce.4.cloned.1.call-update) | async-done | bytes 884752 | tf_op jit(solution)/shard_map/psum | solution.py:84
  845.9 1.8 convolution_maximum_fusion
  847.8 1.5 fusion.41
  849.3 0.6 dynamic-slice.1
  850.5 370.5 %all-gather.7.cloned.1.call-done = f32[110592,128]{1,0:T(8,128)} async-done(((f32[1728,128]{1,0:T(8,128)}), f32[110592,128]{1,0:T(8,128)}) %all-gather.7.cloned.1.call-update) | async-done | bytes 56623120 | tf_op jit(solution)/shard_map/all_gather | solution.py:92
  1221.1 17.9 %reduce_sum.48 = f32[1728,128]{1,0:T(8,128)S(1)} reduce(f32[64,1728,128]{2,1,0:T(8,128)} %bitcast.31, f32[]{:T(128)} %constant.70.clone.1), dimensions={0}, to_apply=%region_7.8 | reduce | flops 13934592 | bytes 57507844 | tf_op jit(solution)/shard_map/reduce_sum | solution.py:92
  1238.9 1.1 fusion.15
  1240.0 8.4 all-reduce.1
  1248.4 0.6 dynamic-slice_bitcast_fusion
  (46 shorter events, 0.8 us)
Async XLA Ops:
  7.2 13.3 %copy-start = (s32[1,8192]{1,0:T(1,128)S(1)}, s32[1,8192]{1,0:T(1,128)}, u32[]{:S(2)}) copy-start(s32[1,8192]{1,0:T(1,128)} %param.11) | copy-start | bytes 98308
  7.2 2.3 copy-start.6
  7.2 2.3 copy-start.5
  7.2 2.4 copy-start.7
  7.2 61.0 %all-gather.5.cloned.1.call-start = ((), (), s32[]{:S(2)}) async-start(), calls=%async_computation | async-start | bytes 2211840 | tf_op jit(solution)/shard_map/all_gather | solution.py:78
  19.5 11.5 copy-start.4
  20.4 825.5 %all-reduce.4.cloned.1.call-start = ((), (), s32[]{:S(2)}) async-start(), calls=%async_computation.1 | async-start | bytes 1769472 | tf_op jit(solution)/shard_map/psum | solution.py:84
  71.3 1149.7 %all-gather.7.cloned.1.call-start = ((), (), s32[]{:S(2)}) async-start(), calls=%async_computation.2 | async-start | bytes 57507840 | tf_op jit(solution)/shard_map/all_gather | solution.py:92
  847.7 391.2 %copy-start.3 = (f32[128,128]{1,0:T(8,128)}, f32[128,128]{1,0:T(8,128)S(1)}, u32[]{:S(2)}) copy-start(f32[128,128]{1,0:T(8,128)S(1)} %convolution_maximum_fusion) | copy-start | bytes 196612
  847.8 1.5 copy-start.8
  1221.1 17.9 %copy-start.2 = (bf16[1728,512]{1,0:T(8,128)(2,1)S(1)}, bf16[1728,512]{1,0:T(8,128)(2,1)}, u32[]{:S(2)}) copy-start(bf16[1728,512]{1,0:T(8,128)(2,1)} %all-gather.5.cloned.1.call-done) | copy-start | bytes 5308420
  1221.1 27.9 %copy-start.1 = (s32[1,8192]{1,0:T(1,128)S(1)}, s32[1,8192]{1,0:T(1,128)}, u32[]{:S(2)}) copy-start(s32[1,8192]{1,0:T(1,128)} %param.11) | copy-start | bytes 98308
Sparse Core Ops, SparseCore 0:
  20.5 47.6 all-gather.4
  71.4 774.4 all-reduce.3
  849.4 371.5 all-gather.6
